TPU v7x, 512 devices: a whole 4x8x8 slice. The times are simulated.
512 devices in a mesh: ctx: 32 (over z, x), tp: 16 (over y, core).
Axes of the slice: x: 4, y: 8, z: 8, core: 2. Of those that a mesh axis runs over, the one named last changes fastest.
Arguments:
- hidden: bfloat16 [8192, 2048], P(('ctx', 'tp')), may hold values from -14 to 14
- in_weight: bfloat16 [2048, 2, 4096], P(None, None, 'tp'), may hold values from -0.125 to 0.125
- step_weight: bfloat16 [2048, 64], P(None, 'tp'), may hold values from -0.125 to 0.125
- group_weight: bfloat16 [256, 4, 2048], P('tp'), may hold values from -0.125 to 0.125
- conv_inner: float32 [4, 4096], P(None, 'tp'), may hold values from -3 to 3
- inner_bias: float32 [4096], P('tp'), may hold values from -2.5 to 2.5
- conv_group: float32 [4, 1024], replicated, may hold values from -3 to 3
- group_bias: float32 [1024], replicated, may hold values from -2.5 to 2.5
- step_bias: float32 [64], P('tp'), may hold values from -9.5 to 0
- log_rate: float32 [64], P('tp'), may hold values from -2.5 to -0.5
- skip_weight: float32 [64], P('tp'), may hold values from 0.25 to 1
- norm_gain: float32 [4096], P('tp'), may hold values from 0.1 to 1.9
- out_weight: bfloat16 [4096, 2048], P('tp'), may hold values from -0.09375 to 0.09375
Outputs:
- mixed: bfloat16 [8192, 2048], P(('ctx', 'tp'))
All inputs are finite; a program needn't handle non-finite values.
Results may differ from a plain program's by a relative error of at most 0.024.
Values may be sent and summed in bfloat16 or wider, within the bound.
No kernel may reach another device: no remote copies, remote signals or barrier semaphores. Data moves between devices by JAX's collectives and lax.ppermute only.
A program may use at most 64 MiB of HBM per device.

v0:
```python
import jax
import jax.numpy as jnp
from jax import lax
from jax.sharding import PartitionSpec as P

HEADS = 64
HEAD_DIM = 64
STATE = 128
GROUPS = 4
BLOCK = 256
KERNEL = 4


def shifted(x, axis, by):
    peers = lax.axis_size(axis)
    pairs = [(i, i + by) for i in range(peers) if 0 <= i + by < peers]
    return lax.ppermute(x, axis, pairs)


def entering(x, axis, combine, identity):
    peers, place = (lax.axis_size(axis), lax.axis_index(axis))
    everything = jax.tree.map(lambda part: lax.all_gather(part, axis), x)
    start = jax.tree.map(
        lambda part, zero: jnp.broadcast_to(jnp.asarray(zero, part.dtype), part.shape), x, identity
    )

    def turn(k, before):
        reached = k < place
        new = combine(before, jax.tree.map(lambda part: part[k], everything))
        return jax.tree.map(lambda a, b: jnp.where(reached, a, b), new, before)

    return lax.fori_loop(0, peers, turn, start)


def causal_conv(prior_rows, raw_rows, conv_weight, conv_bias):
    joined = jnp.concatenate([prior_rows, raw_rows], axis=0).astype(jnp.float32)
    length = raw_rows.shape[0]
    running = jnp.broadcast_to(conv_bias[None, :], raw_rows.shape)
    for offset in range(conv_weight.shape[0]):
        running = running + conv_weight[offset][None, :] * joined[offset : offset + length]
    return jax.nn.silu(running).astype(jnp.bfloat16)


def combine_states(earlier, latter):
    return (earlier[0] * latter[0], latter[0][:, None, None] * earlier[1] + latter[1])


def body(
    hidden,
    in_weight,
    step_weight,
    group_weight,
    conv_inner,
    inner_bias,
    conv_group,
    group_bias,
    step_bias,
    log_rate,
    skip_weight,
    norm_gain,
    out_weight,
):
    heads_dev = log_rate.shape[0]
    inner_dev = in_weight.shape[2]
    group_cols = 2 * STATE
    group_index = lax.axis_index("tp") * heads_dev // (HEADS // GROUPS)
    zx_weight = in_weight.reshape(in_weight.shape[0], 2 * inner_dev)
    full_weight = lax.all_gather(group_weight, "tp", axis=0, tiled=True)
    map_weight = lax.dynamic_slice_in_dim(full_weight, group_index, 1, 1)[:, 0, :]
    shard_rows = lax.all_gather(hidden, "tp", axis=0, tiled=True)
    projected = jnp.concatenate(
        [
            jnp.dot(shard_rows, zx_weight, preferred_element_type=jnp.float32),
            lax.dot_general(
                shard_rows, map_weight, (((1,), (1,)), ((), ())), preferred_element_type=jnp.float32
            ),
            jnp.dot(shard_rows, step_weight, preferred_element_type=jnp.float32),
        ],
        axis=1,
    ).astype(jnp.bfloat16)
    gate_raw = projected[:, :inner_dev]
    inner_raw = projected[:, inner_dev : 2 * inner_dev]
    map_part = projected[:, 2 * inner_dev : projected.shape[1] - heads_dev]
    step_raw = projected[:, projected.shape[1] - heads_dev :]
    border_rows = KERNEL - 1
    length = inner_raw.shape[0]
    inner_prior, map_prior = shifted(
        (inner_raw[length - border_rows :], map_part[length - border_rows :]), "ctx", 1
    )
    x_conv = causal_conv(inner_prior, inner_raw, conv_inner, inner_bias)
    own_taps = lax.dynamic_slice_in_dim(conv_group, group_index * group_cols, group_cols, 1)
    own_bias = lax.dynamic_slice_in_dim(group_bias, group_index * group_cols, group_cols, 0)
    maps = causal_conv(map_prior, map_part, own_taps, own_bias)
    step_size = jax.nn.softplus(step_raw.astype(jnp.float32) + step_bias[None, :])
    decay_rate = -jnp.exp(log_rate)
    blocks = length // BLOCK
    x_blocks = x_conv.reshape(blocks, BLOCK, heads_dev, HEAD_DIM)
    input_map = maps[:, :STATE].reshape(blocks, BLOCK, STATE)
    output_map = maps[:, STATE:].reshape(blocks, BLOCK, STATE)
    step_blocks = jnp.swapaxes(step_size.reshape(blocks, BLOCK, heads_dev), 1, 2)
    cumulative = jnp.cumsum(step_blocks * decay_rate[None, :, None], axis=2)
    scores = jnp.einsum("kin,kjn->kij", output_map, input_map, preferred_element_type=jnp.float32)
    causal = jnp.arange(BLOCK)[:, None] >= jnp.arange(BLOCK)[None, :]
    exponent = jnp.where(causal, cumulative[..., :, None] - cumulative[..., None, :], -jnp.inf)
    mixing = (scores[:, None] * jnp.exp(exponent) * step_blocks[..., None, :]).astype(jnp.bfloat16)
    within = jnp.einsum("khij,kjhp->kihp", mixing, x_blocks, preferred_element_type=jnp.float32)
    weight = jnp.exp(cumulative[..., BLOCK - 1 :] - cumulative) * step_blocks
    x_float = x_blocks.astype(jnp.float32)
    weighted = (x_float * jnp.swapaxes(weight, 1, 2)[..., None]).astype(jnp.bfloat16)
    block_state = jnp.einsum(
        "kjhp,kjn->khpn", weighted, input_map, preferred_element_type=jnp.float32
    )
    block_decay = jnp.exp(cumulative[..., BLOCK - 1])

    def advance(carry, item):
        running, product = carry
        block_stop_index, state_here = item
        return (
            (block_stop_index[:, None, None] * running + state_here, product * block_stop_index),
            (running, product),
        )

    empty_state = jnp.zeros((heads_dev, HEAD_DIM, STATE), jnp.float32)
    (dev_state, dev_decay), (local_starts, prefixes) = lax.scan(
        advance, (empty_state, jnp.ones((heads_dev,), jnp.float32)), (block_decay, block_state)
    )
    decay_in, incoming = entering(
        (dev_decay, dev_state),
        "ctx",
        combine_states,
        (jnp.ones_like(dev_decay), jnp.zeros_like(dev_state)),
    )
    starting = local_starts + prefixes[:, :, None, None] * incoming[None]
    carried = jnp.einsum(
        "kin,khpn->kihp",
        output_map,
        starting.astype(jnp.bfloat16),
        preferred_element_type=jnp.float32,
    )
    carried = carried * jnp.swapaxes(jnp.exp(cumulative), 1, 2)[..., None]
    result_heads = within + carried + skip_weight[None, None, :, None] * x_float
    result_heads = result_heads.reshape(length, inner_dev)
    gated = result_heads * jax.nn.silu(gate_raw.astype(jnp.float32))
    squares = jnp.sum(gated * gated, axis=1)
    own_slot = (jnp.arange(GROUPS) == group_index)[:, None]
    group_sums = lax.psum(jnp.where(own_slot, squares[None, :], 0.0), "tp")
    own_total = jnp.sum(jnp.where(own_slot, group_sums, 0.0), axis=0)
    inverse = lax.rsqrt(own_total / (HEADS * HEAD_DIM // GROUPS) + 1e-05)
    normed = (gated * inverse[:, None] * norm_gain[None, :]).astype(jnp.bfloat16)
    mixed = lax.psum_scatter(
        jnp.dot(normed, out_weight, preferred_element_type=jnp.float32),
        "tp",
        scatter_dimension=0,
        tiled=True,
    )
    return mixed.astype(jnp.bfloat16)


def solution(mesh):
    placed = (
        P(("ctx", "tp"), None),
        P(None, None, "tp"),
        P(None, "tp"),
        P("tp", None, None),
        P(None, "tp"),
        P("tp"),
        P(),
        P(),
        P("tp"),
        P("tp"),
        P("tp"),
        P("tp"),
        P("tp", None),
    )
    return jax.shard_map(
        body, mesh=mesh, in_specs=placed, out_specs=P(("ctx", "tp"), None), check_vma=False
    )
```

profile of v0, /device:TPU:27, one launch (start us, length us, event | category | flops | bytes accessed | tf_op | source)
XLA Modules:
  0.0 323.9 jit_solution(4867282855328708421)
XLA Ops:
  7.3 1.8 copy.45
  9.3 2.1 copy.56
  13.1 41.7 %all-gather.6.cloned.1.call-done = bf16[256,2048]{1,0:T(8,128)(2,1)} async-done(((bf16[16,2048]{1,0:T(8,128)(2,1)}), bf16[256,2048]{1,0:T(8,128)(2,1)}) %all-gather.6.cloned.1.call-update) | async-done | bytes 1048592 | tf_op jit(solution)/shard_map/all_gather | solution.py:70
  54.8 1.6 bitcast_multiply_fusion.1
  56.4 1.2 reduce-window.6
  58.1 1.9 convolution_convert_fusion
  60.1 3.1 collective-permute-start
  64.4 35.8 %all-gather.8.cloned.1.call-done = bf16[256,4,2048]{2,0,1:T(8,128)(2,1)} async-done(((bf16[16,4,2048]{2,0,1:T(8,128)(2,1)}), bf16[256,4,2048]{2,0,1:T(8,128)(2,1)}) %all-gather.8.cloned.1.call-update) | async-done | bytes 4194320 | tf_op jit(solution)/shard_map/all_gather | solution.py:68
  100.3 2.0 fusion.4
  102.3 3.1 collective-permute-start.1
  107.9 34.2 %all-gather = f32[32,4,1]{1,2,0:T(1,128)S(1)} all-gather(f32[1,4,1]{1,2,0:T(1,128)S(1)} %copy.48), channel_id=2, replica_groups=mesh['ctx'=32,'tp'=16] {'ctx'}, dimensions={0}, use_global_device_ids=true | all-gather | bytes 528 | tf_op jit(solution)/shard_map/all_gather | solution.py:22
  142.6 49.1 %all-gather.10.cloned.1.call-done = f32[128,64,128]{2,1,0:T(8,128)} async-done(((f32[4,64,128]{2,1,0:T(8,128)}), f32[128,64,128]{2,1,0:T(8,128)}) %all-gather.10.cloned.1.call-update) | async-done | bytes 4194320 | tf_op jit(solution)/shard_map/all_gather | solution.py:22
  191.7 33.1 %while.9 = (s32[]{:T(128)}, f32[4,64,128]{2,1,0:T(8,128)S(1)}, s32[]{:T(128)}, f32[32,4]{1,0:T(8,128)S(1)}, f32[32,4,64,128]{3,2,1,0:T(8,128)}, /*index=5*/s32[]{:T(128)}, s32[]{:T(128)}) while((s32[]{:T(128)}, f32[4,64,128]{2,1,0:T(8,128)S(1)}, s32[]{:T(128)}, f32[32,4]{1,0:T(8,128)S(1)}, f32[32,4,64,128]{3,2,1,0:T(8,128)}, ...), condition=%wide.region_3.4_spmd.clone, body=%wide.region_2.3_spmd.clone.sunk | while | flops 131076 | bytes 393369 | solution.py:32
  192.7 1.0 fusion.52
  193.8 1.0 fusion.52
  194.8 1.0 fusion.52
  195.8 1.0 fusion.52
  196.9 1.0 fusion.52
  197.9 1.0 fusion.52
  198.9 1.0 fusion.52
  200.0 1.0 fusion.52
  201.0 1.0 fusion.52
  202.0 1.0 fusion.52
  203.1 1.0 fusion.52
  204.1 1.0 fusion.52
  205.1 1.0 fusion.52
  206.2 1.0 fusion.52
  207.2 1.0 fusion.52
  208.2 1.0 fusion.52
  209.3 1.0 fusion.52
  210.3 1.0 fusion.52
  211.3 1.0 fusion.52
  212.4 1.0 fusion.52
  213.4 1.0 fusion.52
  214.5 1.0 fusion.52
  215.5 1.0 fusion.52
  216.5 1.0 fusion.52
  217.6 1.0 fusion.52
  218.6 1.0 fusion.52
  219.6 1.0 fusion.52
  220.7 1.0 fusion.52
  221.7 1.0 fusion.52
  222.7 1.0 fusion.52
  223.8 1.0 fusion.52
  225.8 26.8 %psum.7 = f32[4,256]{1,0:T(4,128)S(1)} all-reduce(f32[4,256]{1,0:T(4,128)S(1)} %broadcast_select_fusion), channel_id=1, replica_groups=mesh['ctx'=32,'tp'=16] {'tp'}, use_global_device_ids=true, to_apply=%region_5.6 | all-reduce | flops 1024 | bytes 8192 | tf_op jit(solution)/shard_map/psum | solution.py:146
  252.8 1.8 fusion.27
  254.7 61.1 %reduce-scatter.2.cloned.1.call-done = f32[16,2048]{1,0:T(8,128)} async-done(((f32[256,2048]{1,0:T(8,128)}), f32[16,2048]{1,0:T(8,128)}) %reduce-scatter.2.cloned.1.call-update) | async-done | bytes 131088 | tf_op jit(solution)/shard_map/reduce_scatter | solution.py:150
  315.8 1.5 convert_element_type.77
  (103 shorter events, 9.5 us)
Async XLA Ops:
  6.5 246.2 %copy-start = (bf16[256,2048]{1,0:T(8,128)(2,1)S(1)}, bf16[256,2048]{1,0:T(8,128)(2,1)}, u32[]{:S(2)}) copy-start(bf16[256,2048]{1,0:T(8,128)(2,1)} %param.27) | copy-start | bytes 3145732
  6.5 48.3 %all-gather.6.cloned.1.call-start = ((), (), s32[]{:S(2)}) async-start(), calls=%async_computation.1 | async-start | bytes 1114112 | tf_op jit(solution)/shard_map/all_gather | solution.py:70
  7.3 93.0 %all-gather.8.cloned.1.call-start = ((), (), s32[]{:S(2)}) async-start(), calls=%async_computation.2 | async-start | bytes 4456448 | tf_op jit(solution)/shard_map/all_gather | solution.py:68
  9.2 182.5 %all-gather.10.cloned.1.call-start = ((), (), s32[]{:S(2)}) async-start(), calls=%async_computation.4 | async-start | bytes 4325376 | tf_op jit(solution)/shard_map/all_gather | solution.py:22
  9.2 3.8 %copy-start.5 = (f32[4]{0:T(128)S(1)}, f32[4]{0:T(128)}, u32[]{:S(2)}) copy-start(f32[4]{0:T(128)} %param.24) | copy-start | bytes 52
  9.2 3.8 %copy-start.1 = (f32[4,256]{1,0:T(4,128)S(1)}, f32[4,256]{1,0:T(4,128)}, u32[]{:S(2)}) copy-start(f32[4,256]{1,0:T(4,128)} %param.19) | copy-start | bytes 12292
  9.3 45.5 %copy-start.4 = (bf16[2048,4]{0,1:T(4,128)(2,1)S(1)}, bf16[2048,4]{0,1:T(4,128)(2,1)}, u32[]{:S(2)}) copy-start(bf16[2048,4]{0,1:T(4,128)(2,1)} %param.17) | copy-start | bytes 49156
  9.3 45.5 %copy-start.6 = (f32[4]{0:T(128)S(1)}, f32[4]{0:T(128)}, u32[]{:S(2)}) copy-start(f32[4]{0:T(128)} %param.23) | copy-start | bytes 52
  60.0 45.4 %copy-start.3 = (f32[256]{0:T(256)S(1)}, f32[256]{0:T(256)}, u32[]{:S(2)}) copy-start(f32[256]{0:T(256)} %param.20) | copy-start | bytes 3076
  60.1 4.3 %collective-permute-start = (bf16[3,256]{1,0:T(4,128)(2,1)S(1)}, bf16[3,256]{1,0:T(4,128)(2,1)S(1)}, u32[]{:S(2)}, u32[]{:S(2)}) collective-permute-start(bf16[3,256]{1,0:T(4,128)(2,1)S(1)} %slice.112), channel_id=1, source_target_pairs={{0,16},{16,32},{32,48},{48,64},{64,80},{80,96},{96,112},{112,128},... | collective-permute-start | bytes 4616 | tf_op jit(solution)/shard_map/ppermute | solution.py:17
  102.3 4.3 %collective-permute-start.1 = (bf16[3,256]{1,0:T(4,128)(2,1)S(1)}, bf16[3,256]{1,0:T(4,128)(2,1)S(1)}, u32[]{:S(2)}, u32[]{:S(2)}) collective-permute-start(bf16[3,256]{1,0:T(4,128)(2,1)S(1)} %slice.118), channel_id=1, source_target_pairs={{0,16},{16,32},{32,48},{48,64},{64,80},{80,96},{96,112},{112,128},... | collective-permute-start | bytes 4616 | tf_op jit(solution)/shard_map/ppermute | solution.py:17
  106.8 118.1 %copy-start.7 = (f32[4]{0:T(128)S(1)}, f32[4]{0:T(128)}, u32[]{:S(2)}) copy-start(f32[4]{0:T(128)} %param.25) | copy-start | bytes 52
  107.7 208.1 %reduce-scatter.2.cloned.1.call-start = ((), (), s32[]{:S(2)}) async-start(), calls=%async_computation.3 | async-start | bytes 2228224 | tf_op jit(solution)/shard_map/reduce_scatter | solution.py:150
  224.8 28.0 %copy-start.2 = (f32[256]{0:T(256)S(1)}, f32[256]{0:T(256)}, u32[]{:S(2)}) copy-start(f32[256]{0:T(256)} %param.26) | copy-start | bytes 3076
Sparse Core Ops, SparseCore 0:
  9.5 45.2 all-gather.5
  56.9 43.2 all-gather.7
  107.8 83.8 all-gather.9
  254.8 60.9 reduce-scatter.1
where the time goes:
time: 325 us; the launch traced here: 324 us
  waiting for transfers between devices  190 us (58%)
  blocking collectives  61.1 us (19%)
  other arithmetic  35.5 us (11%)
  between operations  13.5 us (4%)
  matrix products  9.08 us (3%)
  local copies, waits for them, and re-layouts  7.25 us (2%)
  starting transfers between devices  6.32 us (2%)
    reduce_scatter x1, waiting for transfers between devices, body(): lax.psum_scatter(jnp.dot(normed, out_weight, preferred_element_type=jnp.f...  61.1 us
    all_gather x1, waiting for transfers between devices, entering(): everything = jax.tree.map(lambda part: lax.all_gather(part, axis), x)  49.1 us
    all_gather x1, waiting for transfers between devices, body(): shard_rows = lax.all_gather(hidden, 'tp', axis=0, tiled=True)  41.7 us
    all_gather x1, waiting for transfers between devices, body(): full_weight = lax.all_gather(group_weight, 'tp', axis=0, tiled=True)  35.8 us
    all_gather x1, blocking collectives, entering(): everything = jax.tree.map(lambda part: lax.all_gather(part, axis), x)  34.2 us
    select_n x32, other arithmetic, turn(): return jax.tree.map(lambda a, b: jnp.where(reached, a, b), new, before)  31.8 us
    psum x1, blocking collectives, body(): group_sums = lax.psum(jnp.where(own_slot, squares[None, :], 0.0), 'tp')  26.8 us
  transfers between devices with their start and end apart: 6, of which 6 were waited for; matrix products, arithmetic and copies ran while one was open for 4% of the time, Pallas kernels for 0%

commit v1 on v0

--- a/solution.py
+++ b/solution.py
@@ -67,7 +67,24 @@
     zx_weight = in_weight.reshape(in_weight.shape[0], 2 * inner_dev)
     full_weight = lax.all_gather(group_weight, "tp", axis=0, tiled=True)
     map_weight = lax.dynamic_slice_in_dim(full_weight, group_index, 1, 1)[:, 0, :]
-    shard_rows = lax.all_gather(hidden, "tp", axis=0, tiled=True)
+    length_2, position, extent = (lax.axis_size("tp"), lax.axis_index("tp"), hidden.shape[0])
+    right = [(i_2, (i_2 + 1) % length_2) for i_2 in range(length_2)]
+    backward = [(i_2, (i_2 - 1) % length_2) for i_2 in range(length_2)]
+    out = jnp.zeros((*hidden.shape[:0], length_2 * extent, *hidden.shape[0 + 1 :]), hidden.dtype)
+    out = lax.dynamic_update_slice_in_dim(out, hidden, position * extent, axis=0)
+    from_left = from_right = hidden
+    half = length_2 // 2
+    for step in range(1, half + 1):
+        from_left = lax.ppermute(from_left, "tp", right)
+        out = lax.dynamic_update_slice_in_dim(
+            out, from_left, (position - step) % length_2 * extent, axis=0
+        )
+        if step < length_2 - half:
+            from_right = lax.ppermute(from_right, "tp", backward)
+            out = lax.dynamic_update_slice_in_dim(
+                out, from_right, (position + step) % length_2 * extent, axis=0
+            )
+    shard_rows = out
     projected = jnp.concatenate(
         [
             jnp.dot(shard_rows, zx_weight, preferred_element_type=jnp.float32),

time: 325 us -> 299 us (0.920)
  waiting for transfers between devices: 190 us -> 129 us
  starting transfers between devices: 6.32 us -> 34.2 us
  blocking collectives: 61.1 us -> 67.7 us
    all_gather x1 -> x0, waiting for transfers between devices: 41.7 us -> none  [body(): shard_rows = lax.all_gather(hidden, 'tp', axis=0, tiled=True)]
    all_gather x1, waiting for transfers between devices: 35.8 us -> 0.02 us  [body(): full_weight = lax.all_gather(group_weight, 'tp', axis=0, tiled=True)]
    ppermute x0 -> x15, starting transfers between devices: none -> 27.7 us  [the longest x8 27.7 us: body(): from_left = lax.ppermute(from_left, 'tp', right)]
    ppermute x0 -> x15, waiting for transfers between devices: none -> 12.9 us  [the longest x7 6.92 us: body(): from_right = lax.ppermute(from_right, 'tp', backward)]
    all_gather x1, blocking collectives: 34.2 us -> 40.9 us  [entering(): everything = jax.tree.map(lambda part: lax.all_gather(part, axis), x)]
    all_gather x1, waiting for transfers between devices: 49.1 us -> 53.7 us  [entering(): everything = jax.tree.map(lambda part: lax.all_gather(part, axis), x)]
  transfers between devices with their start and end apart: 6 -> 20, of which waited for: 6 -> 13; matrix products, arithmetic and copies ran while one was open for 4% -> 4% of each run, Pallas kernels for 0% -> 0%
where the time goes in v1:
time: 299 us; the launch traced here: 298 us
  waiting for transfers between devices  129 us (43%)
  blocking collectives  67.7 us (23%)
  other arithmetic  35.5 us (12%)
  starting transfers between devices  34.2 us (11%)
  between operations  13.5 us (5%)
  local copies, waits for them, and re-layouts  9 us (3%)
  matrix products  7.89 us (3%)
    reduce_scatter x1, waiting for transfers between devices, body(): lax.psum_scatter(jnp.dot(normed, out_weight, preferred_element_type=jnp.f...  61.1 us
    all_gather x1, waiting for transfers between devices, entering(): everything = jax.tree.map(lambda part: lax.all_gather(part, axis), x)  53.7 us
    all_gather x1, blocking collectives, entering(): everything = jax.tree.map(lambda part: lax.all_gather(part, axis), x)  40.9 us
    select_n x32, other arithmetic, turn(): return jax.tree.map(lambda a, b: jnp.where(reached, a, b), new, before)  31.8 us
    ppermute x8, starting transfers between devices, body(): from_left = lax.ppermute(from_left, 'tp', right)  27.7 us
    psum x1, blocking collectives, body(): group_sums = lax.psum(jnp.where(own_slot, squares[None, :], 0.0), 'tp')  26.8 us
    ppermute x7, waiting for transfers between devices, body(): from_right = lax.ppermute(from_right, 'tp', backward)  6.92 us
    ppermute x2, starting transfers between devices, shifted(): return lax.ppermute(x, axis, pairs)  6.39 us
  transfers between devices with their start and end apart: 20, of which 13 were waited for; matrix products, arithmetic and copies ran while one was open for 4% of the time, Pallas kernels for 0%

profile of v1, /device:TPU:27, one launch (start us, length us, event | category | flops | bytes accessed | tf_op | source)
XLA Modules:
  0.0 297.9 jit_solution(16449089013121062387)
XLA Ops:
  6.5 1.9 copy.45
  8.5 3.1 %collective-permute-start = (bf16[16,2048]{1,0:T(8,128)(2,1)}, bf16[16,2048]{1,0:T(8,128)(2,1)S(1)}, u32[]{:S(2)}, u32[]{:S(2)}) collective-permute-start(bf16[16,2048]{1,0:T(8,128)(2,1)} %param.15), channel_id=1, source_target_pairs={{0,1},{1,2},{2,3},{3,4},{4,5},{5,6},{6,7},{7,8},{8,9},{9,10},{10,1... | collective-permute-start | bytes 196616 | tf_op jit(solution)/shard_map/ppermute | solution.py:78
  11.6 3.4 %copy.56 = bf16[256,8,2,256]{3,1,2,0:T(8,128)(2,1)} copy(bf16[256,8,2,256]{3,2,1,0:T(2,128)(2,1)} %bitcast.82) | data formatting | bytes 4194304
  16.9 3.0 collective-permute-start.2
  19.9 1.3 collective-permute-done.2
  21.2 3.6 %collective-permute-start.4 = (bf16[16,2048]{1,0:T(8,128)(2,1)S(1)}, bf16[16,2048]{1,0:T(8,128)(2,1)S(1)}, u32[]{:S(2)}, u32[]{:S(2)}) collective-permute-start(bf16[16,2048]{1,0:T(8,128)(2,1)S(1)} %collective-permute-done.2), channel_id=1, source_target_pairs={{0,1},{1,2},{2,3},{3,4},{4,5},{5,6},{6,7},{7,8},{8,9},{9,10},{10,1... | collective-permute-start | bytes 196616 | tf_op jit(solution)/shard_map/ppermute | solution.py:78
  24.8 1.3 collective-permute-done.4
  26.1 3.6 %collective-permute-start.6 = (bf16[16,2048]{1,0:T(8,128)(2,1)S(1)}, bf16[16,2048]{1,0:T(8,128)(2,1)S(1)}, u32[]{:S(2)}, u32[]{:S(2)}) collective-permute-start(bf16[16,2048]{1,0:T(8,128)(2,1)S(1)} %collective-permute-done.4), channel_id=1, source_target_pairs={{0,1},{1,2},{2,3},{3,4},{4,5},{5,6},{6,7},{7,8},{8,9},{9,10},{10,1... | collective-permute-start | bytes 196616 | tf_op jit(solution)/shard_map/ppermute | solution.py:78
  29.7 2.4 collective-permute-done.6
  32.2 3.7 %collective-permute-start.8 = (bf16[16,2048]{1,0:T(8,128)(2,1)S(1)}, bf16[16,2048]{1,0:T(8,128)(2,1)S(1)}, u32[]{:S(2)}, u32[]{:S(2)}) collective-permute-start(bf16[16,2048]{1,0:T(8,128)(2,1)S(1)} %collective-permute-done.6), channel_id=1, source_target_pairs={{0,1},{1,2},{2,3},{3,4},{4,5},{5,6},{6,7},{7,8},{8,9},{9,10},{10,1... | collective-permute-start | bytes 196616 | tf_op jit(solution)/shard_map/ppermute | solution.py:78
  37.2 3.8 %collective-permute-start.10 = (bf16[16,2048]{1,0:T(8,128)(2,1)S(1)}, bf16[16,2048]{1,0:T(8,128)(2,1)S(1)}, u32[]{:S(2)}, u32[]{:S(2)}) collective-permute-start(bf16[16,2048]{1,0:T(8,128)(2,1)S(1)} %collective-permute-done.8), channel_id=1, source_target_pairs={{0,1},{1,2},{2,3},{3,4},{4,5},{5,6},{6,7},{7,8},{8,9},{9,10},{10,1... | collective-permute-start | bytes 196616 | tf_op jit(solution)/shard_map/ppermute | solution.py:78
  41.0 2.0 collective-permute-done.9
  43.1 3.7 %collective-permute-start.12 = (bf16[16,2048]{1,0:T(8,128)(2,1)S(1)}, bf16[16,2048]{1,0:T(8,128)(2,1)S(1)}, u32[]{:S(2)}, u32[]{:S(2)}) collective-permute-start(bf16[16,2048]{1,0:T(8,128)(2,1)S(1)} %collective-permute-done.10), channel_id=1, source_target_pairs={{0,1},{1,2},{2,3},{3,4},{4,5},{5,6},{6,7},{7,8},{8,9},{9,10},{10,1... | collective-permute-start | bytes 196616 | tf_op jit(solution)/shard_map/ppermute | solution.py:78
  46.8 2.3 collective-permute-done.11
  49.2 3.3 %collective-permute-start.14 = (bf16[16,2048]{1,0:T(8,128)(2,1)S(1)}, bf16[16,2048]{1,0:T(8,128)(2,1)S(1)}, u32[]{:S(2)}, u32[]{:S(2)}) collective-permute-start(bf16[16,2048]{1,0:T(8,128)(2,1)S(1)} %collective-permute-done.12), channel_id=1, source_target_pairs={{0,1},{1,2},{2,3},{3,4},{4,5},{5,6},{6,7},{7,8},{8,9},{9,10},{10,1... | collective-permute-start | bytes 196616 | tf_op jit(solution)/shard_map/ppermute | solution.py:78
  52.5 2.1 collective-permute-done.13
  55.2 1.2 reduce-window.6
  56.7 2.3 convolution_convert_fusion
  59.1 3.2 %collective-permute-start.15 = (bf16[3,256]{1,0:T(4,128)(2,1)S(1)}, bf16[3,256]{1,0:T(4,128)(2,1)S(1)}, u32[]{:S(2)}, u32[]{:S(2)}) collective-permute-start(bf16[3,256]{1,0:T(4,128)(2,1)S(1)} %slice.115), channel_id=1, source_target_pairs={{0,16},{16,32},{32,48},{48,64},{64,80},{80,96},{96,112},{112,128},... | collective-permute-start | bytes 4616 | tf_op jit(solution)/shard_map/ppermute | solution.py:17
  63.5 1.7 convolution_convert_fusion.1
  65.2 3.2 %collective-permute-start.16 = (bf16[3,256]{1,0:T(4,128)(2,1)S(1)}, bf16[3,256]{1,0:T(4,128)(2,1)S(1)}, u32[]{:S(2)}, u32[]{:S(2)}) collective-permute-start(bf16[3,256]{1,0:T(4,128)(2,1)S(1)} %slice.121), channel_id=1, source_target_pairs={{0,16},{16,32},{32,48},{48,64},{64,80},{80,96},{96,112},{112,128},... | collective-permute-start | bytes 4616 | tf_op jit(solution)/shard_map/ppermute | solution.py:17
  70.8 40.9 %all-gather = f32[32,4,1]{1,2,0:T(1,128)S(1)} all-gather(f32[1,4,1]{1,2,0:T(1,128)S(1)} %copy.48), channel_id=2, replica_groups=mesh['ctx'=32,'tp'=16] {'ctx'}, dimensions={0}, use_global_device_ids=true | all-gather | bytes 528 | tf_op jit(solution)/shard_map/all_gather | solution.py:22
  112.1 53.7 %all-gather.7.cloned.1.call-done = f32[128,64,128]{2,1,0:T(8,128)} async-done(((f32[4,64,128]{2,1,0:T(8,128)}), f32[128,64,128]{2,1,0:T(8,128)}) %all-gather.7.cloned.1.call-update) | async-done | bytes 4194320 | tf_op jit(solution)/shard_map/all_gather | solution.py:22
  165.8 33.0 %while.9 = (s32[]{:T(128)}, f32[4,64,128]{2,1,0:T(8,128)S(1)}, s32[]{:T(128)}, f32[32,4]{1,0:T(8,128)S(1)}, f32[32,4,64,128]{3,2,1,0:T(8,128)}, /*index=5*/s32[]{:T(128)}, s32[]{:T(128)}) while((s32[]{:T(128)}, f32[4,64,128]{2,1,0:T(8,128)S(1)}, s32[]{:T(128)}, f32[32,4]{1,0:T(8,128)S(1)}, f32[32,4,64,128]{3,2,1,0:T(8,128)}, ...), condition=%wide.region_3.4_spmd.clone, body=%wide.region_2.3_spmd.clone.sunk | while | flops 131076 | bytes 393369 | solution.py:32
  166.8 1.0 fusion.51
  167.9 1.0 fusion.51
  168.9 1.0 fusion.51
  169.9 1.0 fusion.51
  172.0 1.0 fusion.51
  173.0 1.0 fusion.51
  176.1 1.0 fusion.51
  177.2 1.0 fusion.51
  178.2 1.0 fusion.51
  181.3 1.0 fusion.51
  182.3 1.0 fusion.51
  183.4 1.0 fusion.51
  186.5 1.0 fusion.51
  187.5 1.0 fusion.51
  188.5 1.0 fusion.51
  191.6 1.0 fusion.51
  192.7 1.0 fusion.51
  195.8 1.0 fusion.51
  196.8 1.0 fusion.51
  197.8 1.0 fusion.51
  199.9 26.8 %psum.7 = f32[4,256]{1,0:T(4,128)S(1)} all-reduce(f32[4,256]{1,0:T(4,128)S(1)} %broadcast_select_fusion), channel_id=1, replica_groups=mesh['ctx'=32,'tp'=16] {'tp'}, use_global_device_ids=true, to_apply=%region_5.6 | all-reduce | flops 1024 | bytes 8192 | tf_op jit(solution)/shard_map/psum | solution.py:163
  226.9 1.8 fusion.26
  228.7 61.1 %reduce-scatter.2.cloned.1.call-done = f32[16,2048]{1,0:T(8,128)} async-done(((f32[256,2048]{1,0:T(8,128)}), f32[16,2048]{1,0:T(8,128)}) %reduce-scatter.2.cloned.1.call-update) | async-done | bytes 131088 | tf_op jit(solution)/shard_map/reduce_scatter | solution.py:167
  289.9 1.5 convert_element_type.77
  (149 shorter events, 21.6 us)
Async XLA Ops:
  6.5 220.3 %copy-start = (bf16[256,2048]{1,0:T(8,128)(2,1)S(1)}, bf16[256,2048]{1,0:T(8,128)(2,1)}, u32[]{:S(2)}) copy-start(bf16[256,2048]{1,0:T(8,128)(2,1)} %param.27) | copy-start | bytes 3145732
  6.5 56.9 %all-gather.5.cloned.1.call-start = ((), (), s32[]{:S(2)}) async-start(), calls=%async_computation.1 | async-start | bytes 4456448 | tf_op jit(solution)/shard_map/all_gather | solution.py:68
  8.5 157.3 %all-gather.7.cloned.1.call-start = ((), (), s32[]{:S(2)}) async-start(), calls=%async_computation.3 | async-start | bytes 4325376 | tf_op jit(solution)/shard_map/all_gather | solution.py:22
  8.5 8.4 %collective-permute-start = (bf16[16,2048]{1,0:T(8,128)(2,1)}, bf16[16,2048]{1,0:T(8,128)(2,1)S(1)}, u32[]{:S(2)}, u32[]{:S(2)}) collective-permute-start(bf16[16,2048]{1,0:T(8,128)(2,1)} %param.15), channel_id=1, source_target_pairs={{0,1},{1,2},{2,3},{3,4},{4,5},{5,6},{6,7},{7,8},{8,9},{9,10},{10,1... | collective-permute-start | bytes 196616 | tf_op jit(solution)/shard_map/ppermute | solution.py:78
  11.6 8.3 %collective-permute-start.1 = (bf16[16,2048]{1,0:T(8,128)(2,1)}, bf16[16,2048]{1,0:T(8,128)(2,1)S(1)}, u32[]{:S(2)}, u32[]{:S(2)}) collective-permute-start(bf16[16,2048]{1,0:T(8,128)(2,1)} %param.15), channel_id=1, source_target_pairs={{0,15},{1,0},{2,1},{3,2},{4,3},{5,4},{6,5},{7,6},{8,7},{9,8},{10,9... | collective-permute-start | bytes 196616 | tf_op jit(solution)/shard_map/ppermute | solution.py:83
  11.6 4.2 %copy-start.6 = (f32[4]{0:T(128)S(1)}, f32[4]{0:T(128)}, u32[]{:S(2)}) copy-start(f32[4]{0:T(128)} %param.24) | copy-start | bytes 52
  11.6 4.2 %copy-start.2 = (f32[4,256]{1,0:T(4,128)S(1)}, f32[4,256]{1,0:T(4,128)}, u32[]{:S(2)}) copy-start(f32[4,256]{1,0:T(4,128)} %param.19) | copy-start | bytes 12292
  11.6 4.4 %copy-start.1 = (bf16[16,2048]{1,0:T(8,128)(2,1)S(1)}, bf16[16,2048]{1,0:T(8,128)(2,1)}, u32[]{:S(2)}) copy-start(bf16[16,2048]{1,0:T(8,128)(2,1)} %param.15) | copy-start | bytes 196612
  15.0 39.7 %copy-start.5 = (bf16[2048,4]{0,1:T(4,128)(2,1)S(1)}, bf16[2048,4]{0,1:T(4,128)(2,1)}, u32[]{:S(2)}) copy-start(bf16[2048,4]{0,1:T(4,128)(2,1)} %param.17) | copy-start | bytes 49156
  15.0 39.7 %copy-start.7 = (f32[4]{0:T(128)S(1)}, f32[4]{0:T(128)}, u32[]{:S(2)}) copy-start(f32[4]{0:T(128)} %param.23) | copy-start | bytes 52
  16.9 4.3 %collective-permute-start.2 = (bf16[16,2048]{1,0:T(8,128)(2,1)S(1)}, bf16[16,2048]{1,0:T(8,128)(2,1)S(1)}, u32[]{:S(2)}, u32[]{:S(2)}) collective-permute-start(bf16[16,2048]{1,0:T(8,128)(2,1)S(1)} %collective-permute-done), channel_id=1, source_target_pairs={{0,1},{1,2},{2,3},{3,4},{4,5},{5,6},{6,7},{7,8},{8,9},{9,10},{10,1... | collective-permute-start | bytes 196616 | tf_op jit(solution)/shard_map/ppermute | solution.py:78
  19.9 4.9 %collective-permute-start.3 = (bf16[16,2048]{1,0:T(8,128)(2,1)S(1)}, bf16[16,2048]{1,0:T(8,128)(2,1)S(1)}, u32[]{:S(2)}, u32[]{:S(2)}) collective-permute-start(bf16[16,2048]{1,0:T(8,128)(2,1)S(1)} %collective-permute-done.1), channel_id=1, source_target_pairs={{0,15},{1,0},{2,1},{3,2},{4,3},{5,4},{6,5},{7,6},{8,7},{9,8},{10,9... | collective-permute-start | bytes 196616 | tf_op jit(solution)/shard_map/ppermute | solution.py:83
  21.2 4.9 %collective-permute-start.4 = (bf16[16,2048]{1,0:T(8,128)(2,1)S(1)}, bf16[16,2048]{1,0:T(8,128)(2,1)S(1)}, u32[]{:S(2)}, u32[]{:S(2)}) collective-permute-start(bf16[16,2048]{1,0:T(8,128)(2,1)S(1)} %collective-permute-done.2), channel_id=1, source_target_pairs={{0,1},{1,2},{2,3},{3,4},{4,5},{5,6},{6,7},{7,8},{8,9},{9,10},{10,1... | collective-permute-start | bytes 196616 | tf_op jit(solution)/shard_map/ppermute | solution.py:78
  24.8 4.9 %collective-permute-start.5 = (bf16[16,2048]{1,0:T(8,128)(2,1)S(1)}, bf16[16,2048]{1,0:T(8,128)(2,1)S(1)}, u32[]{:S(2)}, u32[]{:S(2)}) collective-permute-start(bf16[16,2048]{1,0:T(8,128)(2,1)S(1)} %collective-permute-done.3), channel_id=1, source_target_pairs={{0,15},{1,0},{2,1},{3,2},{4,3},{5,4},{6,5},{7,6},{8,7},{9,8},{10,9... | collective-permute-start | bytes 196616 | tf_op jit(solution)/shard_map/ppermute | solution.py:83
  26.1 6.0 %collective-permute-start.6 = (bf16[16,2048]{1,0:T(8,128)(2,1)S(1)}, bf16[16,2048]{1,0:T(8,128)(2,1)S(1)}, u32[]{:S(2)}, u32[]{:S(2)}) collective-permute-start(bf16[16,2048]{1,0:T(8,128)(2,1)S(1)} %collective-permute-done.4), channel_id=1, source_target_pairs={{0,1},{1,2},{2,3},{3,4},{4,5},{5,6},{6,7},{7,8},{8,9},{9,10},{10,1... | collective-permute-start | bytes 196616 | tf_op jit(solution)/shard_map/ppermute | solution.py:78
  29.7 6.7 %collective-permute-start.7 = (bf16[16,2048]{1,0:T(8,128)(2,1)S(1)}, bf16[16,2048]{1,0:T(8,128)(2,1)S(1)}, u32[]{:S(2)}, u32[]{:S(2)}) collective-permute-start(bf16[16,2048]{1,0:T(8,128)(2,1)S(1)} %collective-permute-done.5), channel_id=1, source_target_pairs={{0,15},{1,0},{2,1},{3,2},{4,3},{5,4},{6,5},{7,6},{8,7},{9,8},{10,9... | collective-permute-start | bytes 196616 | tf_op jit(solution)/shard_map/ppermute | solution.py:83
  32.2 5.1 %collective-permute-start.8 = (bf16[16,2048]{1,0:T(8,128)(2,1)S(1)}, bf16[16,2048]{1,0:T(8,128)(2,1)S(1)}, u32[]{:S(2)}, u32[]{:S(2)}) collective-permute-start(bf16[16,2048]{1,0:T(8,128)(2,1)S(1)} %collective-permute-done.6), channel_id=1, source_target_pairs={{0,1},{1,2},{2,3},{3,4},{4,5},{5,6},{6,7},{7,8},{8,9},{9,10},{10,1... | collective-permute-start | bytes 196616 | tf_op jit(solution)/shard_map/ppermute | solution.py:78
  36.4 6.6 %collective-permute-start.9 = (bf16[16,2048]{1,0:T(8,128)(2,1)S(1)}, bf16[16,2048]{1,0:T(8,128)(2,1)S(1)}, u32[]{:S(2)}, u32[]{:S(2)}) collective-permute-start(bf16[16,2048]{1,0:T(8,128)(2,1)S(1)} %collective-permute-done.7), channel_id=1, source_target_pairs={{0,15},{1,0},{2,1},{3,2},{4,3},{5,4},{6,5},{7,6},{8,7},{9,8},{10,9... | collective-permute-start | bytes 196616 | tf_op jit(solution)/shard_map/ppermute | solution.py:83
  37.2 5.9 %collective-permute-start.10 = (bf16[16,2048]{1,0:T(8,128)(2,1)S(1)}, bf16[16,2048]{1,0:T(8,128)(2,1)S(1)}, u32[]{:S(2)}, u32[]{:S(2)}) collective-permute-start(bf16[16,2048]{1,0:T(8,128)(2,1)S(1)} %collective-permute-done.8), channel_id=1, source_target_pairs={{0,1},{1,2},{2,3},{3,4},{4,5},{5,6},{6,7},{7,8},{8,9},{9,10},{10,1... | collective-permute-start | bytes 196616 | tf_op jit(solution)/shard_map/ppermute | solution.py:78
  42.9 6.2 %collective-permute-start.11 = (bf16[16,2048]{1,0:T(8,128)(2,1)S(1)}, bf16[16,2048]{1,0:T(8,128)(2,1)S(1)}, u32[]{:S(2)}, u32[]{:S(2)}) collective-permute-start(bf16[16,2048]{1,0:T(8,128)(2,1)S(1)} %collective-permute-done.9), channel_id=1, source_target_pairs={{0,15},{1,0},{2,1},{3,2},{4,3},{5,4},{6,5},{7,6},{8,7},{9,8},{10,9... | collective-permute-start | bytes 196616 | tf_op jit(solution)/shard_map/ppermute | solution.py:83
  43.1 6.0 %collective-permute-start.12 = (bf16[16,2048]{1,0:T(8,128)(2,1)S(1)}, bf16[16,2048]{1,0:T(8,128)(2,1)S(1)}, u32[]{:S(2)}, u32[]{:S(2)}) collective-permute-start(bf16[16,2048]{1,0:T(8,128)(2,1)S(1)} %collective-permute-done.10), channel_id=1, source_target_pairs={{0,1},{1,2},{2,3},{3,4},{4,5},{5,6},{6,7},{7,8},{8,9},{9,10},{10,1... | collective-permute-start | bytes 196616 | tf_op jit(solution)/shard_map/ppermute | solution.py:78
  49.1 5.6 %collective-permute-start.13 = (bf16[16,2048]{1,0:T(8,128)(2,1)S(1)}, bf16[16,2048]{1,0:T(8,128)(2,1)S(1)}, u32[]{:S(2)}, u32[]{:S(2)}) collective-permute-start(bf16[16,2048]{1,0:T(8,128)(2,1)S(1)} %collective-permute-done.11), channel_id=1, source_target_pairs={{0,15},{1,0},{2,1},{3,2},{4,3},{5,4},{6,5},{7,6},{8,7},{9,8},{10,9... | collective-permute-start | bytes 196616 | tf_op jit(solution)/shard_map/ppermute | solution.py:83
  49.2 5.5 %collective-permute-start.14 = (bf16[16,2048]{1,0:T(8,128)(2,1)S(1)}, bf16[16,2048]{1,0:T(8,128)(2,1)S(1)}, u32[]{:S(2)}, u32[]{:S(2)}) collective-permute-start(bf16[16,2048]{1,0:T(8,128)(2,1)S(1)} %collective-permute-done.12), channel_id=1, source_target_pairs={{0,1},{1,2},{2,3},{3,4},{4,5},{5,6},{6,7},{7,8},{8,9},{9,10},{10,1... | collective-permute-start | bytes 196616 | tf_op jit(solution)/shard_map/ppermute | solution.py:78
  59.0 9.3 %copy-start.4 = (f32[256]{0:T(256)S(1)}, f32[256]{0:T(256)}, u32[]{:S(2)}) copy-start(f32[256]{0:T(256)} %param.20) | copy-start | bytes 3076
  59.1 4.3 %collective-permute-start.15 = (bf16[3,256]{1,0:T(4,128)(2,1)S(1)}, bf16[3,256]{1,0:T(4,128)(2,1)S(1)}, u32[]{:S(2)}, u32[]{:S(2)}) collective-permute-start(bf16[3,256]{1,0:T(4,128)(2,1)S(1)} %slice.115), channel_id=1, source_target_pairs={{0,16},{16,32},{32,48},{48,64},{64,80},{80,96},{96,112},{112,128},... | collective-permute-start | bytes 4616 | tf_op jit(solution)/shard_map/ppermute | solution.py:17
  65.2 4.3 %collective-permute-start.16 = (bf16[3,256]{1,0:T(4,128)(2,1)S(1)}, bf16[3,256]{1,0:T(4,128)(2,1)S(1)}, u32[]{:S(2)}, u32[]{:S(2)}) collective-permute-start(bf16[3,256]{1,0:T(4,128)(2,1)S(1)} %slice.121), channel_id=1, source_target_pairs={{0,16},{16,32},{32,48},{48,64},{64,80},{80,96},{96,112},{112,128},... | collective-permute-start | bytes 4616 | tf_op jit(solution)/shard_map/ppermute | solution.py:17
  69.7 129.3 %copy-start.8 = (f32[4]{0:T(128)S(1)}, f32[4]{0:T(128)}, u32[]{:S(2)}) copy-start(f32[4]{0:T(128)} %param.25) | copy-start | bytes 52
  70.6 219.3 %reduce-scatter.2.cloned.1.call-start = ((), (), s32[]{:S(2)}) async-start(), calls=%async_computation.2 | async-start | bytes 2228224 | tf_op jit(solution)/shard_map/reduce_scatter | solution.py:167
  198.9 28.0 %copy-start.3 = (f32[256]{0:T(256)S(1)}, f32[256]{0:T(256)}, u32[]{:S(2)}) copy-start(f32[256]{0:T(256)} %param.26) | copy-start | bytes 3076
Sparse Core Ops, SparseCore 0:
  9.5 49.3 all-gather.4
  70.7 95.0 all-gather.6
  228.8 60.9 reduce-scatter.1
